TPU v7x, 256 devices: a whole 4x4x8 slice. The times are simulated.
256 devices in a mesh: layer: 32 (over z, y), plane: 8 (over x, core).
Axes of the slice: x: 4, y: 4, z: 8, core: 2. Of those that a mesh axis runs over, the one named last changes fastest.
Arguments:
- rhs_field: float32 [32, 2, 4, 64, 1024], P('layer', None, None, None, 'plane'), may hold values from -6 to 6
- panel_inverse: bfloat16 [32, 1024, 2048], P('layer'), may hold values from -1 to 1
- coupling: float32 [32, 2, 4, 64], P('layer', None, None, 'plane'), may hold values from -0.98 to 0.98, as said below
Outputs:
- sweep_field: float32 [32, 2, 4, 64, 1024], P('layer', None, None, None, 'plane')
Inputs may be any that keep to these rules, and one draw needn't show every extreme that they name: Every complex coupling has modulus at most 0.98.
All inputs are finite; a program needn't handle non-finite values.
Results may differ from a plain program's by a relative error of at most 0.025.
Values may be sent and summed in bfloat16 or wider, within the bound.
No kernel may reach another device: no remote copies, remote signals or barrier semaphores. Data moves between devices by JAX's collectives and lax.ppermute only.
A program may use at most 64 MiB of HBM per device.

v0:
```python
import jax
import jax.numpy as jnp
from jax import lax
from jax.sharding import PartitionSpec as P


def from_behind(value, axis, steps):
    count = lax.axis_size(axis)
    first, last = (max(0, -steps), min(count, count - steps))
    return lax.ppermute(value, axis, [(source, source + steps) for source in range(first, last)])


def complex_product(rows, inverse, width):
    flat = rows.reshape(-1, width)
    product = jnp.dot(flat, inverse, preferred_element_type=jnp.float32)
    product = product.reshape(rows.shape[:-1] + (2 * width,))
    real = product[0, ..., :width] - product[1, ..., width:]
    imag = product[0, ..., width:] + product[1, ..., :width]
    return jnp.stack([real, imag])


def twist(factor, field):
    real = factor[0] * field[0] - factor[1] * field[1]
    imag = factor[0] * field[1] + factor[1] * field[0]
    return jnp.stack([real, imag])


def body(rhs_field, panel_inverse, coupling):
    lines = lax.all_to_all(rhs_field, "plane", split_axis=3, concat_axis=4, tiled=True)[0]
    inverse = panel_inverse[0]
    factors = coupling[0][..., None]
    width = inverse.shape[0]
    rhs_count = lines.shape[1]
    per_block = 2
    blocks = rhs_count // per_block
    layers = lax.axis_size("layer")
    place = lax.axis_index("layer")
    sections = layers + blocks - 1
    block_shape = (2, per_block) + lines.shape[2:]
    empty_store = jnp.zeros(lines.shape, jnp.float32)
    empty_block = jnp.zeros(block_shape, jnp.bfloat16)

    def locate(offset):
        valid = (offset >= 0) & (offset < blocks)
        start = jnp.clip(offset, 0, blocks - 1) * per_block
        return (valid, start)

    def forward(section, carry):
        store, outgoing = carry
        incoming = from_behind(outgoing, "layer", 1)
        valid, start = locate(section - place)
        source = lax.dynamic_slice_in_dim(lines, start, per_block, 1)
        factor = lax.dynamic_slice_in_dim(factors, start, per_block, 1)
        mixed = (source + twist(factor, incoming.astype(jnp.float32))).astype(jnp.bfloat16)
        result = complex_product(mixed, inverse, width)
        previous = lax.dynamic_slice_in_dim(store, start, per_block, 1)
        store = lax.dynamic_update_slice_in_dim(store, jnp.where(valid, result, previous), start, 1)
        return (store, result.astype(jnp.bfloat16))

    forward_store, _ = lax.fori_loop(0, sections, forward, (empty_store, empty_block))

    def backward(section, carry):
        store, outgoing = carry
        incoming = from_behind(outgoing, "layer", -1)
        valid, start = locate(section - (layers - 1 - place))
        starting_position = lax.dynamic_slice_in_dim(forward_store, start, per_block, 1)
        factor = lax.dynamic_slice_in_dim(factors, start, per_block, 1)
        result = starting_position + complex_product(incoming, inverse, width)
        previous = lax.dynamic_slice_in_dim(store, start, per_block, 1)
        store = lax.dynamic_update_slice_in_dim(store, jnp.where(valid, result, previous), start, 1)
        return (store, twist(factor, result).astype(jnp.bfloat16))

    backward_store, _ = lax.fori_loop(0, sections, backward, (empty_store, empty_block))
    return lax.all_to_all(backward_store[None], "plane", split_axis=4, concat_axis=3, tiled=True)


def solution(mesh):
    in_specs = (
        P("layer", None, None, None, "plane"),
        P("layer", None, None),
        P("layer", None, None, "plane"),
    )
    out_specs = P("layer", None, None, None, "plane")
    return jax.shard_map(body, mesh=mesh, in_specs=in_specs, out_specs=out_specs, check_vma=False)
```

profile of v0, /device:TPU:120, one launch (start us, length us, event | category | flops | bytes accessed | tf_op | source)
XLA Modules:
  0.0 887.2 jit_solution(6325632736517630927)
XLA Ops:
  13.7 417.3 %while.34 = (s32[]{:T(128)}, f32[2,4,8,1024]{3,2,1,0:T(8,128)S(1)}, bf16[2,2,8,1024]{3,2,1,0:T(8,128)(2,1)S(1)}, s32[]{:T(128)}, f32[2,4,8,1024]{3,2,1,0:T(8,128...) while((s32[]{:T(128)}, f32[2,4,8,1024]{3,2,1,0:T(8,128)S(1)}, ...), condition=%wide.region_1.2_spmd.clone, body=%wide.region_0.1_spmd.clone.sunk | while | flops 134610960 | bytes 6554283 | solution.py:60
  23.5 7.6 collective-permute-start.1
  36.2 7.6 collective-permute-start.1
  48.9 7.6 collective-permute-start.1
  61.6 7.6 collective-permute-start.1
  74.3 7.6 collective-permute-start.1
  87.0 7.6 collective-permute-start.1
  99.7 7.6 collective-permute-start.1
  112.4 7.6 collective-permute-start.1
  125.1 7.6 collective-permute-start.1
  138.0 7.7 collective-permute-start.1
  150.8 7.6 collective-permute-start.1
  163.5 7.6 collective-permute-start.1
  176.2 7.6 collective-permute-start.1
  188.9 7.6 collective-permute-start.1
  201.6 7.6 collective-permute-start.1
  214.3 7.6 collective-permute-start.1
  227.0 7.6 collective-permute-start.1
  239.6 7.6 collective-permute-start.1
  252.3 7.6 collective-permute-start.1
  265.6 7.7 collective-permute-start.1
  278.4 7.6 collective-permute-start.1
  291.1 7.6 collective-permute-start.1
  316.5 7.6 collective-permute-start.1
  329.1 7.6 collective-permute-start.1
  354.5 7.6 collective-permute-start.1
  367.2 7.6 collective-permute-start.1
  379.9 7.6 collective-permute-start.1
  392.8 7.7 collective-permute-start.1
  418.3 7.6 collective-permute-start.1
  431.0 418.7 %while.33 = (s32[]{:T(128)}, f32[2,4,8,1024]{3,2,1,0:T(8,128)S(1)}, bf16[2,2,8,1024]{3,2,1,0:T(8,128)(2,1)S(1)}, s32[]{:T(128)}, f32[2,4,8,1024]{3,2,1,0:T(8,128...) while((s32[]{:T(128)}, f32[2,4,8,1024]{3,2,1,0:T(8,128)S(1)}, ...), condition=%wide.region_3.4_spmd, body=%wide.region_2.3_spmd.sunk | while | flops 134512656 | bytes 6161053 | solution.py:73
  864.2 9.9 %all_to_all.33 = f32[8,1,8192]{2,1,0:T(1,128)S(1)} all-to-all(f32[8,1,8192]{2,1,0:T(1,128)S(1)} %reshape.23), channel_id=1, replica_groups=mesh['layer'=32,'plane'=8] {'plane'}, dimensions={0} | all-to-all | bytes 524288 | tf_op jit(solution)/shard_map/all_to_all | solution.py:74
  (580 shorter events, 651.9 us)
Async XLA Ops:
  1.8 11.8 %all-to-all-start = ((f32[1,2,4,64,128]{4,2,1,0,3:T(4,128)}), f32[1,2,4,64,128]{4,2,1,0,3:T(4,128)S(1)}, u32[]{:S(2)}, u32[]{:S(2)}) async-start(f32[1,2,4,64,128]{4,2,1,0,3:T(4,128)} %copy.6), calls=%async_computation | async-start | bytes 524288 | tf_op jit(solution)/shard_map/all_to_all | solution.py:29
  23.5 9.5 %collective-permute-start.1 = (bf16[2,2,8,1024]{3,2,1,0:T(8,128)(2,1)S(1)}, bf16[2,2,8,1024]{3,2,1,0:T(8,128)(2,1)S(1)}, u32[]{:S(2)}, u32[]{:S(2)}) collective-permute-start(bf16[2,2,8,1024]{3,2,1,0:T(8,128)(2,1)S(1)} %broadcast_select_fusion.2), channel_id=1, source_target_pairs={{0,8},{8,16},{16,24},{24,32},{32,40},{40,48},{48,56},{56,64},{64,7... | collective-permute-start | bytes 196616 | tf_op jit(solution)/shard_map/while/body/eval_jaxpr/ppermute | solution.py:10
  36.2 9.5 %collective-permute-start.1 = (bf16[2,2,8,1024]{3,2,1,0:T(8,128)(2,1)S(1)}, bf16[2,2,8,1024]{3,2,1,0:T(8,128)(2,1)S(1)}, u32[]{:S(2)}, u32[]{:S(2)}) collective-permute-start(bf16[2,2,8,1024]{3,2,1,0:T(8,128)(2,1)S(1)} %broadcast_select_fusion.2), channel_id=1, source_target_pairs={{0,8},{8,16},{16,24},{24,32},{32,40},{40,48},{48,56},{56,64},{64,7... | collective-permute-start | bytes 196616 | tf_op jit(solution)/shard_map/while/body/eval_jaxpr/ppermute | solution.py:10
  48.9 9.5 %collective-permute-start.1 = (bf16[2,2,8,1024]{3,2,1,0:T(8,128)(2,1)S(1)}, bf16[2,2,8,1024]{3,2,1,0:T(8,128)(2,1)S(1)}, u32[]{:S(2)}, u32[]{:S(2)}) collective-permute-start(bf16[2,2,8,1024]{3,2,1,0:T(8,128)(2,1)S(1)} %broadcast_select_fusion.2), channel_id=1, source_target_pairs={{0,8},{8,16},{16,24},{24,32},{32,40},{40,48},{48,56},{56,64},{64,7... | collective-permute-start | bytes 196616 | tf_op jit(solution)/shard_map/while/body/eval_jaxpr/ppermute | solution.py:10
  61.6 9.5 %collective-permute-start.1 = (bf16[2,2,8,1024]{3,2,1,0:T(8,128)(2,1)S(1)}, bf16[2,2,8,1024]{3,2,1,0:T(8,128)(2,1)S(1)}, u32[]{:S(2)}, u32[]{:S(2)}) collective-permute-start(bf16[2,2,8,1024]{3,2,1,0:T(8,128)(2,1)S(1)} %broadcast_select_fusion.2), channel_id=1, source_target_pairs={{0,8},{8,16},{16,24},{24,32},{32,40},{40,48},{48,56},{56,64},{64,7... | collective-permute-start | bytes 196616 | tf_op jit(solution)/shard_map/while/body/eval_jaxpr/ppermute | solution.py:10
  74.3 9.5 %collective-permute-start.1 = (bf16[2,2,8,1024]{3,2,1,0:T(8,128)(2,1)S(1)}, bf16[2,2,8,1024]{3,2,1,0:T(8,128)(2,1)S(1)}, u32[]{:S(2)}, u32[]{:S(2)}) collective-permute-start(bf16[2,2,8,1024]{3,2,1,0:T(8,128)(2,1)S(1)} %broadcast_select_fusion.2), channel_id=1, source_target_pairs={{0,8},{8,16},{16,24},{24,32},{32,40},{40,48},{48,56},{56,64},{64,7... | collective-permute-start | bytes 196616 | tf_op jit(solution)/shard_map/while/body/eval_jaxpr/ppermute | solution.py:10
  87.0 9.5 %collective-permute-start.1 = (bf16[2,2,8,1024]{3,2,1,0:T(8,128)(2,1)S(1)}, bf16[2,2,8,1024]{3,2,1,0:T(8,128)(2,1)S(1)}, u32[]{:S(2)}, u32[]{:S(2)}) collective-permute-start(bf16[2,2,8,1024]{3,2,1,0:T(8,128)(2,1)S(1)} %broadcast_select_fusion.2), channel_id=1, source_target_pairs={{0,8},{8,16},{16,24},{24,32},{32,40},{40,48},{48,56},{56,64},{64,7... | collective-permute-start | bytes 196616 | tf_op jit(solution)/shard_map/while/body/eval_jaxpr/ppermute | solution.py:10
  99.7 9.5 %collective-permute-start.1 = (bf16[2,2,8,1024]{3,2,1,0:T(8,128)(2,1)S(1)}, bf16[2,2,8,1024]{3,2,1,0:T(8,128)(2,1)S(1)}, u32[]{:S(2)}, u32[]{:S(2)}) collective-permute-start(bf16[2,2,8,1024]{3,2,1,0:T(8,128)(2,1)S(1)} %broadcast_select_fusion.2), channel_id=1, source_target_pairs={{0,8},{8,16},{16,24},{24,32},{32,40},{40,48},{48,56},{56,64},{64,7... | collective-permute-start | bytes 196616 | tf_op jit(solution)/shard_map/while/body/eval_jaxpr/ppermute | solution.py:10
  112.4 9.5 %collective-permute-start.1 = (bf16[2,2,8,1024]{3,2,1,0:T(8,128)(2,1)S(1)}, bf16[2,2,8,1024]{3,2,1,0:T(8,128)(2,1)S(1)}, u32[]{:S(2)}, u32[]{:S(2)}) collective-permute-start(bf16[2,2,8,1024]{3,2,1,0:T(8,128)(2,1)S(1)} %broadcast_select_fusion.2), channel_id=1, source_target_pairs={{0,8},{8,16},{16,24},{24,32},{32,40},{40,48},{48,56},{56,64},{64,7... | collective-permute-start | bytes 196616 | tf_op jit(solution)/shard_map/while/body/eval_jaxpr/ppermute | solution.py:10
  125.1 9.8 %collective-permute-start.1 = (bf16[2,2,8,1024]{3,2,1,0:T(8,128)(2,1)S(1)}, bf16[2,2,8,1024]{3,2,1,0:T(8,128)(2,1)S(1)}, u32[]{:S(2)}, u32[]{:S(2)}) collective-permute-start(bf16[2,2,8,1024]{3,2,1,0:T(8,128)(2,1)S(1)} %broadcast_select_fusion.2), channel_id=1, source_target_pairs={{0,8},{8,16},{16,24},{24,32},{32,40},{40,48},{48,56},{56,64},{64,7... | collective-permute-start | bytes 196616 | tf_op jit(solution)/shard_map/while/body/eval_jaxpr/ppermute | solution.py:10
  138.0 9.6 %collective-permute-start.1 = (bf16[2,2,8,1024]{3,2,1,0:T(8,128)(2,1)S(1)}, bf16[2,2,8,1024]{3,2,1,0:T(8,128)(2,1)S(1)}, u32[]{:S(2)}, u32[]{:S(2)}) collective-permute-start(bf16[2,2,8,1024]{3,2,1,0:T(8,128)(2,1)S(1)} %broadcast_select_fusion.2), channel_id=1, source_target_pairs={{0,8},{8,16},{16,24},{24,32},{32,40},{40,48},{48,56},{56,64},{64,7... | collective-permute-start | bytes 196616 | tf_op jit(solution)/shard_map/while/body/eval_jaxpr/ppermute | solution.py:10
  150.8 9.5 %collective-permute-start.1 = (bf16[2,2,8,1024]{3,2,1,0:T(8,128)(2,1)S(1)}, bf16[2,2,8,1024]{3,2,1,0:T(8,128)(2,1)S(1)}, u32[]{:S(2)}, u32[]{:S(2)}) collective-permute-start(bf16[2,2,8,1024]{3,2,1,0:T(8,128)(2,1)S(1)} %broadcast_select_fusion.2), channel_id=1, source_target_pairs={{0,8},{8,16},{16,24},{24,32},{32,40},{40,48},{48,56},{56,64},{64,7... | collective-permute-start | bytes 196616 | tf_op jit(solution)/shard_map/while/body/eval_jaxpr/ppermute | solution.py:10
  163.5 9.5 %collective-permute-start.1 = (bf16[2,2,8,1024]{3,2,1,0:T(8,128)(2,1)S(1)}, bf16[2,2,8,1024]{3,2,1,0:T(8,128)(2,1)S(1)}, u32[]{:S(2)}, u32[]{:S(2)}) collective-permute-start(bf16[2,2,8,1024]{3,2,1,0:T(8,128)(2,1)S(1)} %broadcast_select_fusion.2), channel_id=1, source_target_pairs={{0,8},{8,16},{16,24},{24,32},{32,40},{40,48},{48,56},{56,64},{64,7... | collective-permute-start | bytes 196616 | tf_op jit(solution)/shard_map/while/body/eval_jaxpr/ppermute | solution.py:10
  176.2 9.5 %collective-permute-start.1 = (bf16[2,2,8,1024]{3,2,1,0:T(8,128)(2,1)S(1)}, bf16[2,2,8,1024]{3,2,1,0:T(8,128)(2,1)S(1)}, u32[]{:S(2)}, u32[]{:S(2)}) collective-permute-start(bf16[2,2,8,1024]{3,2,1,0:T(8,128)(2,1)S(1)} %broadcast_select_fusion.2), channel_id=1, source_target_pairs={{0,8},{8,16},{16,24},{24,32},{32,40},{40,48},{48,56},{56,64},{64,7... | collective-permute-start | bytes 196616 | tf_op jit(solution)/shard_map/while/body/eval_jaxpr/ppermute | solution.py:10
  188.9 9.5 %collective-permute-start.1 = (bf16[2,2,8,1024]{3,2,1,0:T(8,128)(2,1)S(1)}, bf16[2,2,8,1024]{3,2,1,0:T(8,128)(2,1)S(1)}, u32[]{:S(2)}, u32[]{:S(2)}) collective-permute-start(bf16[2,2,8,1024]{3,2,1,0:T(8,128)(2,1)S(1)} %broadcast_select_fusion.2), channel_id=1, source_target_pairs={{0,8},{8,16},{16,24},{24,32},{32,40},{40,48},{48,56},{56,64},{64,7... | collective-permute-start | bytes 196616 | tf_op jit(solution)/shard_map/while/body/eval_jaxpr/ppermute | solution.py:10
  201.6 9.5 %collective-permute-start.1 = (bf16[2,2,8,1024]{3,2,1,0:T(8,128)(2,1)S(1)}, bf16[2,2,8,1024]{3,2,1,0:T(8,128)(2,1)S(1)}, u32[]{:S(2)}, u32[]{:S(2)}) collective-permute-start(bf16[2,2,8,1024]{3,2,1,0:T(8,128)(2,1)S(1)} %broadcast_select_fusion.2), channel_id=1, source_target_pairs={{0,8},{8,16},{16,24},{24,32},{32,40},{40,48},{48,56},{56,64},{64,7... | collective-permute-start | bytes 196616 | tf_op jit(solution)/shard_map/while/body/eval_jaxpr/ppermute | solution.py:10
  227.0 9.5 %collective-permute-start.1 = (bf16[2,2,8,1024]{3,2,1,0:T(8,128)(2,1)S(1)}, bf16[2,2,8,1024]{3,2,1,0:T(8,128)(2,1)S(1)}, u32[]{:S(2)}, u32[]{:S(2)}) collective-permute-start(bf16[2,2,8,1024]{3,2,1,0:T(8,128)(2,1)S(1)} %broadcast_select_fusion.2), channel_id=1, source_target_pairs={{0,8},{8,16},{16,24},{24,32},{32,40},{40,48},{48,56},{56,64},{64,7... | collective-permute-start | bytes 196616 | tf_op jit(solution)/shard_map/while/body/eval_jaxpr/ppermute | solution.py:10
  239.6 9.5 %collective-permute-start.1 = (bf16[2,2,8,1024]{3,2,1,0:T(8,128)(2,1)S(1)}, bf16[2,2,8,1024]{3,2,1,0:T(8,128)(2,1)S(1)}, u32[]{:S(2)}, u32[]{:S(2)}) collective-permute-start(bf16[2,2,8,1024]{3,2,1,0:T(8,128)(2,1)S(1)} %broadcast_select_fusion.2), channel_id=1, source_target_pairs={{0,8},{8,16},{16,24},{24,32},{32,40},{40,48},{48,56},{56,64},{64,7... | collective-permute-start | bytes 196616 | tf_op jit(solution)/shard_map/while/body/eval_jaxpr/ppermute | solution.py:10
  252.3 10.0 %collective-permute-start.1 = (bf16[2,2,8,1024]{3,2,1,0:T(8,128)(2,1)S(1)}, bf16[2,2,8,1024]{3,2,1,0:T(8,128)(2,1)S(1)}, u32[]{:S(2)}, u32[]{:S(2)}) collective-permute-start(bf16[2,2,8,1024]{3,2,1,0:T(8,128)(2,1)S(1)} %broadcast_select_fusion.2), channel_id=1, source_target_pairs={{0,8},{8,16},{16,24},{24,32},{32,40},{40,48},{48,56},{56,64},{64,7... | collective-permute-start | bytes 196616 | tf_op jit(solution)/shard_map/while/body/eval_jaxpr/ppermute | solution.py:10
  265.6 9.6 %collective-permute-start.1 = (bf16[2,2,8,1024]{3,2,1,0:T(8,128)(2,1)S(1)}, bf16[2,2,8,1024]{3,2,1,0:T(8,128)(2,1)S(1)}, u32[]{:S(2)}, u32[]{:S(2)}) collective-permute-start(bf16[2,2,8,1024]{3,2,1,0:T(8,128)(2,1)S(1)} %broadcast_select_fusion.2), channel_id=1, source_target_pairs={{0,8},{8,16},{16,24},{24,32},{32,40},{40,48},{48,56},{56,64},{64,7... | collective-permute-start | bytes 196616 | tf_op jit(solution)/shard_map/while/body/eval_jaxpr/ppermute | solution.py:10
  278.4 9.5 %collective-permute-start.1 = (bf16[2,2,8,1024]{3,2,1,0:T(8,128)(2,1)S(1)}, bf16[2,2,8,1024]{3,2,1,0:T(8,128)(2,1)S(1)}, u32[]{:S(2)}, u32[]{:S(2)}) collective-permute-start(bf16[2,2,8,1024]{3,2,1,0:T(8,128)(2,1)S(1)} %broadcast_select_fusion.2), channel_id=1, source_target_pairs={{0,8},{8,16},{16,24},{24,32},{32,40},{40,48},{48,56},{56,64},{64,7... | collective-permute-start | bytes 196616 | tf_op jit(solution)/shard_map/while/body/eval_jaxpr/ppermute | solution.py:10
  316.5 9.5 %collective-permute-start.1 = (bf16[2,2,8,1024]{3,2,1,0:T(8,128)(2,1)S(1)}, bf16[2,2,8,1024]{3,2,1,0:T(8,128)(2,1)S(1)}, u32[]{:S(2)}, u32[]{:S(2)}) collective-permute-start(bf16[2,2,8,1024]{3,2,1,0:T(8,128)(2,1)S(1)} %broadcast_select_fusion.2), channel_id=1, source_target_pairs={{0,8},{8,16},{16,24},{24,32},{32,40},{40,48},{48,56},{56,64},{64,7... | collective-permute-start | bytes 196616 | tf_op jit(solution)/shard_map/while/body/eval_jaxpr/ppermute | solution.py:10
  329.1 9.5 %collective-permute-start.1 = (bf16[2,2,8,1024]{3,2,1,0:T(8,128)(2,1)S(1)}, bf16[2,2,8,1024]{3,2,1,0:T(8,128)(2,1)S(1)}, u32[]{:S(2)}, u32[]{:S(2)}) collective-permute-start(bf16[2,2,8,1024]{3,2,1,0:T(8,128)(2,1)S(1)} %broadcast_select_fusion.2), channel_id=1, source_target_pairs={{0,8},{8,16},{16,24},{24,32},{32,40},{40,48},{48,56},{56,64},{64,7... | collective-permute-start | bytes 196616 | tf_op jit(solution)/shard_map/while/body/eval_jaxpr/ppermute | solution.py:10
  354.5 9.5 %collective-permute-start.1 = (bf16[2,2,8,1024]{3,2,1,0:T(8,128)(2,1)S(1)}, bf16[2,2,8,1024]{3,2,1,0:T(8,128)(2,1)S(1)}, u32[]{:S(2)}, u32[]{:S(2)}) collective-permute-start(bf16[2,2,8,1024]{3,2,1,0:T(8,128)(2,1)S(1)} %broadcast_select_fusion.2), channel_id=1, source_target_pairs={{0,8},{8,16},{16,24},{24,32},{32,40},{40,48},{48,56},{56,64},{64,7... | collective-permute-start | bytes 196616 | tf_op jit(solution)/shard_map/while/body/eval_jaxpr/ppermute | solution.py:10
  367.2 9.5 %collective-permute-start.1 = (bf16[2,2,8,1024]{3,2,1,0:T(8,128)(2,1)S(1)}, bf16[2,2,8,1024]{3,2,1,0:T(8,128)(2,1)S(1)}, u32[]{:S(2)}, u32[]{:S(2)}) collective-permute-start(bf16[2,2,8,1024]{3,2,1,0:T(8,128)(2,1)S(1)} %broadcast_select_fusion.2), channel_id=1, source_target_pairs={{0,8},{8,16},{16,24},{24,32},{32,40},{40,48},{48,56},{56,64},{64,7... | collective-permute-start | bytes 196616 | tf_op jit(solution)/shard_map/while/body/eval_jaxpr/ppermute | solution.py:10
  379.9 9.7 %collective-permute-start.1 = (bf16[2,2,8,1024]{3,2,1,0:T(8,128)(2,1)S(1)}, bf16[2,2,8,1024]{3,2,1,0:T(8,128)(2,1)S(1)}, u32[]{:S(2)}, u32[]{:S(2)}) collective-permute-start(bf16[2,2,8,1024]{3,2,1,0:T(8,128)(2,1)S(1)} %broadcast_select_fusion.2), channel_id=1, source_target_pairs={{0,8},{8,16},{16,24},{24,32},{32,40},{40,48},{48,56},{56,64},{64,7... | collective-permute-start | bytes 196616 | tf_op jit(solution)/shard_map/while/body/eval_jaxpr/ppermute | solution.py:10
  392.8 9.6 %collective-permute-start.1 = (bf16[2,2,8,1024]{3,2,1,0:T(8,128)(2,1)S(1)}, bf16[2,2,8,1024]{3,2,1,0:T(8,128)(2,1)S(1)}, u32[]{:S(2)}, u32[]{:S(2)}) collective-permute-start(bf16[2,2,8,1024]{3,2,1,0:T(8,128)(2,1)S(1)} %broadcast_select_fusion.2), channel_id=1, source_target_pairs={{0,8},{8,16},{16,24},{24,32},{32,40},{40,48},{48,56},{56,64},{64,7... | collective-permute-start | bytes 196616 | tf_op jit(solution)/shard_map/while/body/eval_jaxpr/ppermute | solution.py:10
  418.3 9.5 %collective-permute-start.1 = (bf16[2,2,8,1024]{3,2,1,0:T(8,128)(2,1)S(1)}, bf16[2,2,8,1024]{3,2,1,0:T(8,128)(2,1)S(1)}, u32[]{:S(2)}, u32[]{:S(2)}) collective-permute-start(bf16[2,2,8,1024]{3,2,1,0:T(8,128)(2,1)S(1)} %broadcast_select_fusion.2), channel_id=1, source_target_pairs={{0,8},{8,16},{16,24},{24,32},{32,40},{40,48},{48,56},{56,64},{64,7... | collective-permute-start | bytes 196616 | tf_op jit(solution)/shard_map/while/body/eval_jaxpr/ppermute | solution.py:10
  431.0 9.8 %collective-permute-start = (bf16[2,2,8,1024]{3,2,1,0:T(8,128)(2,1)S(1)}, bf16[2,2,8,1024]{3,2,1,0:T(8,128)(2,1)S(1)}, u32[]{:S(2)}, u32[]{:S(2)}) collective-permute-start(bf16[2,2,8,1024]{3,2,1,0:T(8,128)(2,1)S(1)} %get-tuple-element.559), channel_id=1, source_target_pairs={{8,0},{16,8},{24,16},{32,24},{40,32},{48,40},{56,48},{64,56},{72,6... | collective-permute-start | bytes 196616 | tf_op jit(solution)/shard_map/while/body/eval_jaxpr/ppermute | solution.py:10
  507.3 9.6 %collective-permute-start = (bf16[2,2,8,1024]{3,2,1,0:T(8,128)(2,1)S(1)}, bf16[2,2,8,1024]{3,2,1,0:T(8,128)(2,1)S(1)}, u32[]{:S(2)}, u32[]{:S(2)}) collective-permute-start(bf16[2,2,8,1024]{3,2,1,0:T(8,128)(2,1)S(1)} %get-tuple-element.559), channel_id=1, source_target_pairs={{8,0},{16,8},{24,16},{32,24},{40,32},{48,40},{56,48},{64,56},{72,6... | collective-permute-start | bytes 196616 | tf_op jit(solution)/shard_map/while/body/eval_jaxpr/ppermute | solution.py:10
  520.1 9.6 %collective-permute-start = (bf16[2,2,8,1024]{3,2,1,0:T(8,128)(2,1)S(1)}, bf16[2,2,8,1024]{3,2,1,0:T(8,128)(2,1)S(1)}, u32[]{:S(2)}, u32[]{:S(2)}) collective-permute-start(bf16[2,2,8,1024]{3,2,1,0:T(8,128)(2,1)S(1)} %get-tuple-element.559), channel_id=1, source_target_pairs={{8,0},{16,8},{24,16},{32,24},{40,32},{48,40},{56,48},{64,56},{72,6... | collective-permute-start | bytes 196616 | tf_op jit(solution)/shard_map/while/body/eval_jaxpr/ppermute | solution.py:10
  646.8 9.9 %collective-permute-start = (bf16[2,2,8,1024]{3,2,1,0:T(8,128)(2,1)S(1)}, bf16[2,2,8,1024]{3,2,1,0:T(8,128)(2,1)S(1)}, u32[]{:S(2)}, u32[]{:S(2)}) collective-permute-start(bf16[2,2,8,1024]{3,2,1,0:T(8,128)(2,1)S(1)} %get-tuple-element.559), channel_id=1, source_target_pairs={{8,0},{16,8},{24,16},{32,24},{40,32},{48,40},{56,48},{64,56},{72,6... | collective-permute-start | bytes 196616 | tf_op jit(solution)/shard_map/while/body/eval_jaxpr/ppermute | solution.py:10
  (35 other events, 328.9 us)
where the time goes:
time: 893 us; the launch traced here: 887 us
  starting transfers between devices  316 us (35%)
  waiting for transfers between devices  273 us (31%)
  matrix products  197 us (22%)
  local copies, waits for them, and re-layouts  75 us (8%)
  other arithmetic  11.8 us (1%)
  blocking collectives  9.91 us (1%)
    ppermute x66, starting transfers between devices, from_behind(): lax.ppermute(value, axis, [(source, source + steps) for source in range(f...  311 us
    ppermute x66, waiting for transfers between devices, from_behind(): lax.ppermute(value, axis, [(source, source + steps) for source in range(f...  265 us
    dot_general x66, matrix products, complex_product(): product = jnp.dot(flat, inverse, preferred_element_type=jnp.float32)  197 us
    mul x66, local copies, waits for them, and re-layouts, twist(): real = factor[0] * field[0] - factor[1] * field[1]  46.8 us
    unnamed x4, local copies, waits for them, and re-layouts  20.1 us
  transfers between devices with their start and end apart: 67, of which 67 were waited for; matrix products, arithmetic and copies ran while one was open for 5% of the time, Pallas kernels for 0%

commit v1 on v0

v1 whole, which is shorter than its diff:
```python
import jax
import jax.numpy as jnp
from jax import lax
from jax.sharding import PartitionSpec as P


def complex_product(rows, inverse, width):
    flat = rows.reshape(-1, width)
    product = jnp.dot(flat, inverse, preferred_element_type=jnp.float32)
    product = product.reshape(rows.shape[:-1] + (2 * width,))
    real = product[0, ..., :width] - product[1, ..., width:]
    imag = product[0, ..., width:] + product[1, ..., :width]
    return jnp.stack([real, imag])


def twist(factor, field):
    real = factor[0] * field[0] - factor[1] * field[1]
    imag = factor[0] * field[1] + factor[1] * field[0]
    return jnp.stack([real, imag])


def body(rhs_field, panel_inverse, coupling):
    lines = lax.all_to_all(rhs_field, "plane", split_axis=3, concat_axis=4, tiled=True)[0]
    inverse = panel_inverse[0]
    factors = coupling[0][..., None]
    width = inverse.shape[0]
    layers = lax.axis_size("layer")
    planes = lax.axis_size("plane")
    place = lax.axis_index("layer")
    plane = lax.axis_index("plane")
    pairs = layers // 2
    down = [(2 * j + 1, 2 * j) for j in range(pairs)]
    ahead = [(2 * j, 2 * j + 2) for j in range(pairs - 1)]
    behind = [(2 * j + 2, 2 * j) for j in range(pairs - 1)]
    back = [(2 * j, 2 * j + 1) for j in range(pairs)]

    rows = width // planes
    piece = lax.dynamic_slice_in_dim(inverse, plane * rows, rows, 0)
    piece = lax.ppermute(piece, "layer", down)
    inverse_next = lax.all_gather(piece, "plane", axis=0, tiled=True)
    lines_next = lax.ppermute(lines, "layer", down)
    factors_next = lax.ppermute(factors, "layer", down)

    def pair_forward(incoming):
        mixed = (lines + twist(factors, incoming.astype(jnp.float32))).astype(jnp.bfloat16)
        first = complex_product(mixed, inverse, width)
        carried = first.astype(jnp.bfloat16).astype(jnp.float32)
        mixed = (lines_next + twist(factors_next, carried)).astype(jnp.bfloat16)
        second = complex_product(mixed, inverse_next, width)
        return first, second

    first, second = pair_forward(jnp.zeros(lines.shape, jnp.bfloat16))
    valid = place == 0
    store_a = jnp.where(valid, first, 0.0)
    store_b = jnp.where(valid, second, 0.0)

    def forward(section, carry):
        store_a, store_b, outgoing = carry
        incoming = lax.ppermute(outgoing, "layer", ahead)
        first, second = pair_forward(incoming)
        valid = place == 2 * section
        store_a = jnp.where(valid, first, store_a)
        store_b = jnp.where(valid, second, store_b)
        return (store_a, store_b, second.astype(jnp.bfloat16))

    store_a, store_b, _ = lax.fori_loop(1, pairs, forward, (store_a, store_b, second.astype(jnp.bfloat16)))

    def pair_backward(sweep_b):
        carried = twist(factors_next, sweep_b).astype(jnp.bfloat16)
        sweep_a = store_a + complex_product(carried, inverse, width)
        return sweep_a, twist(factors, sweep_a).astype(jnp.bfloat16)

    sweep_b = store_b
    sweep_a, outgoing = pair_backward(sweep_b)
    valid = place == layers - 2
    result_a = jnp.where(valid, sweep_a, 0.0)
    result_b = jnp.where(valid, sweep_b, 0.0)

    def backward(section, carry):
        result_a, result_b, outgoing = carry
        incoming = lax.ppermute(outgoing, "layer", behind)
        sweep_b = store_b + complex_product(incoming, inverse_next, width)
        sweep_a, outgoing = pair_backward(sweep_b)
        valid = place == layers - 2 - 2 * section
        result_a = jnp.where(valid, sweep_a, result_a)
        result_b = jnp.where(valid, sweep_b, result_b)
        return (result_a, result_b, outgoing)

    result_a, result_b, _ = lax.fori_loop(1, pairs, backward, (result_a, result_b, outgoing))
    returned = lax.ppermute(result_b, "layer", back)
    result = jnp.where(place % 2 == 0, result_a, returned)
    return lax.all_to_all(result[None], "plane", split_axis=4, concat_axis=3, tiled=True)


def solution(mesh):
    in_specs = (
        P("layer", None, None, None, "plane"),
        P("layer", None, None),
        P("layer", None, None, "plane"),
    )
    out_specs = P("layer", None, None, None, "plane")
    return jax.shard_map(body, mesh=mesh, in_specs=in_specs, out_specs=out_specs, check_vma=False)
```

time: 893 us -> 570 us (0.64)
  starting transfers between devices: 316 us -> 37.1 us
  matrix products: 197 us -> 130 us
  waiting for transfers between devices: 273 us -> 329 us
  local copies, waits for them, and re-layouts: 75 us -> 27.3 us
  between operations: 0.06 us -> 13.6 us
    ppermute x66 -> x34, starting transfers between devices: 311 us -> 32.8 us  [the longest x15 10 us: forward(): incoming = lax.ppermute(outgoing, 'layer', ahead)]
    dot_general x66 -> x63, matrix products: 197 us -> 130 us  [complex_product(): product = jnp.dot(flat, inverse, preferred_element_type=jnp.float32)]
    ppermute x66 -> x34, waiting for transfers between devices: 265 us -> 313 us  [the longest x1 299 us: body(): returned = lax.ppermute(result_b, 'layer', back)]
    mul x66 -> x48, local copies, waits for them, and re-layouts: 46.8 us -> 0.93 us  [twist(): real = factor[0] * field[0] - factor[1] * field[1]]
    all_gather x0 -> x1, waiting for transfers between devices: none -> 14.8 us  [body(): inverse_next = lax.all_gather(piece, 'plane', axis=0, tiled=True)]
    unnamed x4 -> x7, local copies, waits for them, and re-layouts: 20.1 us -> 16.1 us
  transfers between devices with their start and end apart: 67 -> 36, of which waited for: 67 -> 6; matrix products, arithmetic and copies ran while one was open for 5% -> 1% of each run, Pallas kernels for 0% -> 0%
where the time goes in v1:
time: 570 us; the launch traced here: 569 us
  waiting for transfers between devices  329 us (58%)
  matrix products  130 us (23%)
  starting transfers between devices  37.1 us (7%)
  local copies, waits for them, and re-layouts  27.3 us (5%)
  other arithmetic  17.9 us (3%)
  between operations  13.6 us (2%)
  blocking collectives  10.3 us (2%)
    ppermute x1, waiting for transfers between devices, body(): returned = lax.ppermute(result_b, 'layer', back)  299 us
    dot_general x63, matrix products, complex_product(): product = jnp.dot(flat, inverse, preferred_element_type=jnp.float32)  130 us
    unnamed x7, local copies, waits for them, and re-layouts  16.1 us
    all_gather x1, waiting for transfers between devices, body(): inverse_next = lax.all_gather(piece, 'plane', axis=0, tiled=True)  14.8 us
  transfers between devices with their start and end apart: 36, of which 6 were waited for; matrix products, arithmetic and copies ran while one was open for 1% of the time, Pallas kernels for 0%

profile of v1, /device:TPU:120, one launch (start us, length us, event | category | flops | bytes accessed | tf_op | source)
XLA Modules:
  0.0 568.8 jit_solution(8651485035003527377)
XLA Ops:
  10.3 11.1 %collective-permute-done.4 = bf16[128,2048]{1,0:T(8,128)(2,1)S(1)} collective-permute-done((bf16[128,2048]{1,0:T(8,128)(2,1)S(1)}, bf16[128,2048]{1,0:T(8,128)(2,1)S(1)}, u32[]{:S(2)}, u32[]{:S(2)}) %collective-permute-start.4) | collective-permute-done | bytes 524320 | tf_op jit(solution)/shard_map/ppermute | solution.py:39
  24.1 4.3 all-to-all-start
  28.4 4.4 collective-permute-start.3
  36.0 4.4 collective-permute-start.2
  45.5 14.8 %all-gather.2.cloned.1.call-done = bf16[1024,2048]{1,0:T(8,128)(2,1)} async-done(((bf16[128,2048]{1,0:T(8,128)(2,1)}), bf16[1024,2048]{1,0:T(8,128)(2,1)}) %all-gather.2.cloned.1.call-update) | async-done | bytes 4194320 | tf_op jit(solution)/shard_map/all_gather | solution.py:40
  63.5 80.7 %while.34 = (s32[]{:T(128)}, f32[2,4,8,1024]{3,2,1,0:T(8,128)S(1)}, f32[2,4,8,1024]{3,2,1,0:T(8,128)S(1)}, bf16[2,4,8,1024]{3,2,1,0:T(8,128)(2,1)S(1)}, s32[]{:T...) while((s32[]{:T(128)}, f32[2,4,8,1024]{3,2,1,0:T(8,128)S(1)}, ...), condition=%wide.region_1.2_spmd, body=%wide.region_0.1_spmd.sunk | while | flops 538312704 | bytes 33294036 | solution.py:66
  64.3 3.2 fusion.65
  69.7 3.2 fusion.65
  75.1 3.2 fusion.65
  80.5 3.2 fusion.65
  85.9 3.2 fusion.65
  91.3 3.2 fusion.65
  96.6 3.2 fusion.65
  102.0 3.2 fusion.65
  107.4 3.2 fusion.65
  112.8 3.2 fusion.65
  118.2 3.2 fusion.65
  123.5 3.2 fusion.65
  128.9 3.2 fusion.65
  134.3 3.2 fusion.65
  139.7 3.2 fusion.65
  147.6 80.6 %while.35 = (s32[]{:T(128)}, f32[2,4,8,1024]{3,2,1,0:T(8,128)S(1)}, f32[2,4,8,1024]{3,2,1,0:T(8,128)S(1)}, bf16[2,4,8,1024]{3,2,1,0:T(8,128)(2,1)S(1)}, s32[]{:T...) while((s32[]{:T(128)}, f32[2,4,8,1024]{3,2,1,0:T(8,128)S(1)}, ...), condition=%wide.region_3.4_spmd, body=%wide.region_2.3_spmd.sunk | while | flops 538050560 | bytes 32245480 | solution.py:89
  148.3 3.2 fusion.74
  153.7 3.2 fusion.74
  159.1 3.2 fusion.74
  164.4 3.2 fusion.74
  175.2 3.2 fusion.74
  229.5 299.4 %collective-permute-done.5 = f32[2,4,8,1024]{3,2,1,0:T(8,128)S(1)} collective-permute-done((f32[2,4,8,1024]{3,2,1,0:T(8,128)S(1)}, f32[2,4,8,1024]{3,2,1,0:T(8,128)S(1)}, u32[]{:S(2)}, u32[]{:S(2)}) %collective-permute-start.5) | collective-permute-done | bytes 262176 | tf_op jit(solution)/shard_map/ppermute | solution.py:90
  532.0 6.5 %reshape.75 = f32[8,1,8192]{2,1,0:T(1,128)S(1)} reshape(f32[1024,1,2,4,8]{4,3,2,1,0:T(4,128)} %bitcast.114) | data formatting | bytes 524288
  538.6 10.3 %all_to_all.33 = f32[8,1,8192]{2,1,0:T(1,128)S(1)} all-to-all(f32[8,1,8192]{2,1,0:T(1,128)S(1)} %reshape.75), channel_id=1, replica_groups=mesh['layer'=32,'plane'=8] {'plane'}, dimensions={0} | all-to-all | bytes 524288 | tf_op jit(solution)/shard_map/all_to_all | solution.py:92
  550.6 6.9 %reshape.76 = f32[1024,1,2,4,8]{4,3,2,1,0:T(4,128)} reshape(f32[8,8192]{1,0:T(8,128)S(1)} %reduce) | data formatting | bytes 524288
  557.5 4.4 copy.24
  (468 shorter events, 121.3 us)
Async XLA Ops:
  6.5 53.8 %all-gather.2.cloned.1.call-start = ((), (), s32[]{:S(2)}) async-start(), calls=%async_computation.2 | async-start | bytes 4718592 | tf_op jit(solution)/shard_map/all_gather | solution.py:40
  7.6 13.8 %collective-permute-start.4 = (bf16[128,2048]{1,0:T(8,128)(2,1)S(1)}, bf16[128,2048]{1,0:T(8,128)(2,1)S(1)}, u32[]{:S(2)}, u32[]{:S(2)}) collective-permute-start(bf16[128,2048]{1,0:T(8,128)(2,1)S(1)} %dynamic-slice_bitcast_fusion), channel_id=1, source_target_pairs={{8,0},{24,16},{40,32},{56,48},{72,64},{88,80},{104,96},{120,112},{... | collective-permute-start | bytes 1572872 | tf_op jit(solution)/shard_map/ppermute | solution.py:39
  24.1 11.8 %all-to-all-start = ((f32[1,2,4,64,128]{4,2,1,0,3:T(4,128)}), f32[1,2,4,64,128]{4,2,1,0,3:T(4,128)S(1)}, u32[]{:S(2)}, u32[]{:S(2)}) async-start(f32[1,2,4,64,128]{4,2,1,0,3:T(4,128)} %copy.17), calls=%async_computation | async-start | bytes 524288 | tf_op jit(solution)/shard_map/all_to_all | solution.py:23
  28.4 5.9 %collective-permute-start.3 = (f32[2,4,8,1]{2,1,0,3:T(4,128)}, f32[2,4,8,1]{2,1,0,3:T(4,128)S(1)}, u32[]{:S(2)}, u32[]{:S(2)}) collective-permute-start(f32[2,4,8,1]{2,1,0,3:T(4,128)} %bitcast.120), channel_id=1, source_target_pairs={{8,0},{24,16},{40,32},{56,48},{72,64},{88,80},{104,96},{120,112},{... | collective-permute-start | bytes 776 | tf_op jit(solution)/shard_map/ppermute | solution.py:42
  36.0 9.6 %collective-permute-start.2 = (f32[2,4,8,1024]{3,2,1,0:T(8,128)S(1)}, f32[2,4,8,1024]{3,2,1,0:T(8,128)S(1)}, u32[]{:S(2)}, u32[]{:S(2)}) collective-permute-start(f32[2,4,8,1024]{3,2,1,0:T(8,128)S(1)} %bitcast.116), channel_id=1, source_target_pairs={{8,0},{24,16},{40,32},{56,48},{72,64},{88,80},{104,96},{120,112},{... | collective-permute-start | bytes 786440 | tf_op jit(solution)/shard_map/ppermute | solution.py:41
  63.5 0.7 collective-permute-start
  68.9 0.7 collective-permute-start
  74.2 0.7 collective-permute-start
  79.6 0.7 collective-permute-start
  85.0 0.7 collective-permute-start
  90.4 0.7 collective-permute-start
  95.8 0.7 collective-permute-start
  101.2 0.7 collective-permute-start
  106.5 0.7 collective-permute-start
  111.9 0.7 collective-permute-start
  117.3 0.7 collective-permute-start
  122.7 0.7 collective-permute-start
  128.1 0.7 collective-permute-start
  133.4 0.7 collective-permute-start
  138.8 0.7 collective-permute-start
  147.6 0.7 collective-permute-start.1
  153.0 0.7 collective-permute-start.1
  158.4 0.7 collective-permute-start.1
  163.7 0.7 collective-permute-start.1
  169.1 0.7 collective-permute-start.1
  174.5 0.7 collective-permute-start.1
  179.8 0.7 collective-permute-start.1
  185.2 0.7 collective-permute-start.1
  190.6 0.7 collective-permute-start.1
  201.3 0.7 collective-permute-start.1
  206.7 0.7 collective-permute-start.1
  228.2 300.8 %collective-permute-start.5 = (f32[2,4,8,1024]{3,2,1,0:T(8,128)S(1)}, f32[2,4,8,1024]{3,2,1,0:T(8,128)S(1)}, u32[]{:S(2)}, u32[]{:S(2)}) collective-permute-start(f32[2,4,8,1024]{3,2,1,0:T(8,128)S(1)} %get-tuple-element.378), channel_id=1, source_target_pairs={{0,8},{16,24},{32,40},{48,56},{64,72},{80,88},{96,104},{112,120},{... | collective-permute-start | bytes 786440 | tf_op jit(solution)/shard_map/ppermute | solution.py:90
  (36 other events, 127.5 us)
Sparse Core Ops, SparseCore 0:
  22.4 37.9 all-gather.1

commit v2 on v1

--- a/solution.py
+++ b/solution.py
@@ -30,8 +30,6 @@
     plane = lax.axis_index("plane")
     pairs = layers // 2
     down = [(2 * j + 1, 2 * j) for j in range(pairs)]
-    ahead = [(2 * j, 2 * j + 2) for j in range(pairs - 1)]
-    behind = [(2 * j + 2, 2 * j) for j in range(pairs - 1)]
     back = [(2 * j, 2 * j + 1) for j in range(pairs)]
 
     rows = width // planes
@@ -49,44 +47,52 @@
         second = complex_product(mixed, inverse_next, width)
         return first, second
 
-    first, second = pair_forward(jnp.zeros(lines.shape, jnp.bfloat16))
-    valid = place == 0
-    store_a = jnp.where(valid, first, 0.0)
-    store_b = jnp.where(valid, second, 0.0)
+    zeros = jnp.zeros(lines.shape, jnp.float32)
+    outgoing = jnp.zeros(lines.shape, jnp.bfloat16)
+    store_a, store_b = zeros, zeros
+    for section in range(pairs):
+        if section > 0:
+            incoming = lax.ppermute(outgoing, "layer", [(2 * section - 2, 2 * section)])
+        else:
+            incoming = outgoing
 
-    def forward(section, carry):
-        store_a, store_b, outgoing = carry
-        incoming = lax.ppermute(outgoing, "layer", ahead)
-        first, second = pair_forward(incoming)
-        valid = place == 2 * section
-        store_a = jnp.where(valid, first, store_a)
-        store_b = jnp.where(valid, second, store_b)
-        return (store_a, store_b, second.astype(jnp.bfloat16))
+        def active(incoming, store_a, store_b, outgoing):
+            first, second = pair_forward(incoming)
+            return first, second, second.astype(jnp.bfloat16)
 
-    store_a, store_b, _ = lax.fori_loop(1, pairs, forward, (store_a, store_b, second.astype(jnp.bfloat16)))
+        def idle(incoming, store_a, store_b, outgoing):
+            return store_a, store_b, outgoing
+
+        store_a, store_b, outgoing = lax.cond(
+            place == 2 * section, active, idle, incoming, store_a, store_b, outgoing)
 
     def pair_backward(sweep_b):
         carried = twist(factors_next, sweep_b).astype(jnp.bfloat16)
         sweep_a = store_a + complex_product(carried, inverse, width)
         return sweep_a, twist(factors, sweep_a).astype(jnp.bfloat16)
 
-    sweep_b = store_b
-    sweep_a, outgoing = pair_backward(sweep_b)
-    valid = place == layers - 2
-    result_a = jnp.where(valid, sweep_a, 0.0)
-    result_b = jnp.where(valid, sweep_b, 0.0)
+    result_a, result_b = zeros, zeros
+    for section in range(pairs):
+        lead = layers - 2 - 2 * section
+        if section > 0:
+            incoming = lax.ppermute(outgoing, "layer", [(lead + 2, lead)])
+        else:
+            incoming = outgoing
 
-    def backward(section, carry):
-        result_a, result_b, outgoing = carry
-        incoming = lax.ppermute(outgoing, "layer", behind)
-        sweep_b = store_b + complex_product(incoming, inverse_next, width)
-        sweep_a, outgoing = pair_backward(sweep_b)
-        valid = place == layers - 2 - 2 * section
-        result_a = jnp.where(valid, sweep_a, result_a)
-        result_b = jnp.where(valid, sweep_b, result_b)
-        return (result_a, result_b, outgoing)
+        def active(incoming, result_a, result_b, outgoing, first=(section == 0)):
+            if first:
+                sweep_b = store_b
+            else:
+                sweep_b = store_b + complex_product(incoming, inverse_next, width)
+            sweep_a, outgoing = pair_backward(sweep_b)
+            return sweep_a, sweep_b, outgoing
 
-    result_a, result_b, _ = lax.fori_loop(1, pairs, backward, (result_a, result_b, outgoing))
+        def idle(incoming, result_a, result_b, outgoing):
+            return result_a, result_b, outgoing
+
+        result_a, result_b, outgoing = lax.cond(
+            place == lead, active, idle, incoming, result_a, result_b, outgoing)
+
     returned = lax.ppermute(result_b, "layer", back)
     result = jnp.where(place % 2 == 0, result_a, returned)
     return lax.all_to_all(result[None], "plane", split_axis=4, concat_axis=3, tiled=True)

time: 570 us -> 514 us (0.902)
  the two profiles are of different devices: /device:TPU:120 before, /device:TPU:8 now
where the time goes in v2:
time: 514 us; the launch traced here: 504 us
  waiting for transfers between devices  399 us (78%)
  starting transfers between devices  31.6 us (6%)
  local copies, waits for them, and re-layouts  26.1 us (5%)
  blocking collectives  22.6 us (4%)
  between operations  14.7 us (3%)
  loops' own time  8.44 us (2%)
    ppermute x1, waiting for transfers between devices, body(): returned = lax.ppermute(result_b, 'layer', back)  369 us
    all_gather x1, waiting for transfers between devices, body(): inverse_next = lax.all_gather(piece, 'plane', axis=0, tiled=True)  17.2 us
    unnamed x5, local copies, waits for them, and re-layouts  15.4 us
    all_to_all x1, blocking collectives, body(): lax.all_to_all(rhs_field, 'plane', split_axis=3, concat_axis=4, tiled=True)  12.4 us
    ppermute x15, starting transfers between devices, body(): incoming = lax.ppermute(outgoing, 'layer', [(2 * section - 2, 2 * section)])  10.5 us
  transfers between devices with their start and end apart: 35, of which 4 were waited for; matrix products, arithmetic and copies ran while one was open for 0% of the time, Pallas kernels for 0%

profile of v2, /device:TPU:8, one launch (start us, length us, event | category | flops | bytes accessed | tf_op | source)
XLA Modules:
  0.0 503.9 jit_solution(14405069978480361503)
XLA Ops:
  6.5 1.1 dynamic-slice_bitcast_fusion
  7.6 4.1 collective-permute-start.2
  11.7 8.6 %collective-permute-done.2 = bf16[128,2048]{1,0:T(8,128)(2,1)S(1)} collective-permute-done((bf16[128,2048]{1,0:T(8,128)(2,1)S(1)}, bf16[128,2048]{1,0:T(8,128)(2,1)S(1)}, u32[]{:S(2)}, u32[]{:S(2)}) %collective-permute-start.2) | collective-permute-done | bytes 524320 | tf_op jit(solution)/shard_map/ppermute | solution.py:37
  20.4 0.8 copy-done.46
  21.2 1.1 copy.135
  22.3 12.4 %all_to_all.33 = f32[1,2,4,64,128]{4,2,1,0,3:T(4,128)S(1)} all-to-all(f32[1,2,4,64,128]{4,2,1,0,3:T(4,128)S(1)} %copy.135), channel_id=1, replica_groups=mesh['layer'=32,'plane'=8] {'plane'}, dimensions={3} | all-to-all | bytes 524288 | tf_op jit(solution)/shard_map/all_to_all | solution.py:23
  34.8 4.4 collective-permute-start.1
  39.2 1.3 collective-permute-start
  40.5 3.9 collective-permute-done
  44.4 17.2 %all-gather.2.cloned.1.call-done = bf16[1024,2048]{1,0:T(8,128)(2,1)} async-done(((bf16[128,2048]{1,0:T(8,128)(2,1)}), bf16[1024,2048]{1,0:T(8,128)(2,1)}) %all-gather.2.cloned.1.call-update) | async-done | bytes 4194320 | tf_op jit(solution)/shard_map/all_gather | solution.py:38
  62.4 0.7 collective-permute-start.4
  64.5 0.7 collective-permute-start.7
  65.2 0.7 collective-permute-start.8
  65.9 1.1 collective-permute-start.9
  67.8 0.7 collective-permute-start.11
  69.9 0.7 collective-permute-start.14
  70.6 0.7 collective-permute-start.15
  72.0 3.5 conditional.46
  75.5 0.7 collective-permute-start.17
  76.2 1.5 conditional.48
  76.3 0.7 broadcast_in_dim.10
  77.0 0.7 broadcast_in_dim.10.clone
  81.9 1.6 conditional.54
  88.4 3.1 conditional.61
  93.0 1.3 collective-permute-start.33
  94.3 369.3 %collective-permute-done.33 = f32[2,4,8,1024]{3,2,1,0:T(8,128)S(1)} collective-permute-done((f32[2,4,8,1024]{3,2,1,0:T(8,128)}, f32[2,4,8,1024]{3,2,1,0:T(8,128)S(1)}, u32[]{:S(2)}, u32[]{:S(2)}) %collective-permute-start.33) | collective-permute-done | bytes 262176 | tf_op jit(solution)/shard_map/ppermute | solution.py:96
  463.6 3.1 copy.200
  466.7 6.5 %reshape.449 = f32[8,1,8192]{2,1,0:T(1,128)S(1)} reshape(f32[1024,1,2,4,8]{4,3,2,1,0:T(4,128)} %bitcast.712) | data formatting | bytes 524288
  473.3 10.2 %all_to_all.34 = f32[8,1,8192]{2,1,0:T(1,128)S(1)} all-to-all(f32[8,1,8192]{2,1,0:T(1,128)S(1)} %reshape.449), channel_id=1, replica_groups=mesh['layer'=32,'plane'=8] {'plane'}, dimensions={0} | all-to-all | bytes 524288 | tf_op jit(solution)/shard_map/all_to_all | solution.py:98
  484.0 1.3 reduce
  485.3 7.0 %reshape.450 = f32[1024,1,2,4,8]{4,3,2,1,0:T(4,128)} reshape(f32[8,8192]{1,0:T(8,128)S(1)} %reduce) | data formatting | bytes 524288
  492.3 4.4 copy.201
  (90 shorter events, 15.7 us)
Async XLA Ops:
  6.5 55.1 %all-gather.2.cloned.1.call-start = ((), (), s32[]{:S(2)}) async-start(), calls=%async_computation.2 | async-start | bytes 4718592 | tf_op jit(solution)/shard_map/all_gather | solution.py:38
  7.6 12.7 %collective-permute-start.2 = (bf16[128,2048]{1,0:T(8,128)(2,1)S(1)}, bf16[128,2048]{1,0:T(8,128)(2,1)S(1)}, u32[]{:S(2)}, u32[]{:S(2)}) collective-permute-start(bf16[128,2048]{1,0:T(8,128)(2,1)S(1)} %dynamic-slice_bitcast_fusion), channel_id=1, source_target_pairs={{8,0},{24,16},{40,32},{56,48},{72,64},{88,80},{104,96},{120,112},{... | collective-permute-start | bytes 1572872 | tf_op jit(solution)/shard_map/ppermute | solution.py:37
  34.8 9.7 %collective-permute-start.1 = (f32[2,4,8,1024]{3,2,1,0:T(8,128)S(1)}, f32[2,4,8,1024]{3,2,1,0:T(8,128)S(1)}, u32[]{:S(2)}, u32[]{:S(2)}) collective-permute-start(f32[2,4,8,1024]{3,2,1,0:T(8,128)S(1)} %bitcast.695), channel_id=1, source_target_pairs={{8,0},{24,16},{40,32},{56,48},{72,64},{88,80},{104,96},{120,112},{... | collective-permute-start | bytes 786440 | tf_op jit(solution)/shard_map/ppermute | solution.py:39
  39.2 5.3 %collective-permute-start = (f32[2,4,8,1]{2,1,0,3:T(4,128)}, f32[2,4,8,1]{2,1,0,3:T(4,128)S(1)}, u32[]{:S(2)}, u32[]{:S(2)}) collective-permute-start(f32[2,4,8,1]{2,1,0,3:T(4,128)} %bitcast.746), channel_id=1, source_target_pairs={{8,0},{24,16},{40,32},{56,48},{72,64},{88,80},{104,96},{120,112},{... | collective-permute-start | bytes 776 | tf_op jit(solution)/shard_map/ppermute | solution.py:40
  61.7 0.7 collective-permute-start.3
  62.4 0.7 collective-permute-start.4
  63.1 0.7 collective-permute-start.5
  63.8 0.7 collective-permute-start.6
  64.5 0.7 collective-permute-start.7
  65.2 0.7 collective-permute-start.8
  65.9 1.1 collective-permute-start.9
  67.1 0.7 collective-permute-start.10
  67.8 0.7 collective-permute-start.11
  68.5 0.7 collective-permute-start.12
  69.2 0.7 collective-permute-start.13
  69.9 0.7 collective-permute-start.14
  70.6 0.7 collective-permute-start.15
  71.4 0.7 collective-permute-start.16
  75.5 0.7 collective-permute-start.17
  78.4 0.7 collective-permute-start.19
  79.1 0.7 collective-permute-start.20
  79.8 0.7 collective-permute-start.21
  80.5 0.7 collective-permute-start.22
  81.2 0.7 collective-permute-start.23
  83.5 0.7 collective-permute-start.24
  84.2 0.7 collective-permute-start.25
  85.6 0.7 collective-permute-start.27
  86.3 0.7 collective-permute-start.28
  87.0 0.7 collective-permute-start.29
  87.7 0.7 collective-permute-start.30
  92.3 0.7 collective-permute-start.32
  93.0 370.6 %collective-permute-start.33 = (f32[2,4,8,1024]{3,2,1,0:T(8,128)}, f32[2,4,8,1024]{3,2,1,0:T(8,128)S(1)}, u32[]{:S(2)}, u32[]{:S(2)}) collective-permute-start(f32[2,4,8,1024]{3,2,1,0:T(8,128)} %get-tuple-element.921), channel_id=1, source_target_pairs={{0,8},{16,24},{32,40},{48,56},{64,72},{80,88},{96,104},{112,120},{... | collective-permute-start | bytes 786440 | tf_op jit(solution)/shard_map/ppermute | solution.py:96
  (4 other events, 2.8 us)
Sparse Core Ops, SparseCore 0:
  21.3 40.2 all-gather.1

commit v3 on v2

v3 whole, which is shorter than its diff:
```python
import jax
import jax.numpy as jnp
from jax import lax
from jax.sharding import PartitionSpec as P


def complex_product(real, imag, inverse):
    width = inverse.shape[0]
    rows = jnp.stack([real, imag])
    flat = rows.reshape(-1, width)
    product = jnp.dot(flat, inverse, preferred_element_type=jnp.float32)
    product = product.reshape(rows.shape[:-1] + (2 * width,))
    return (product[0, ..., :width] - product[1, ..., width:],
            product[0, ..., width:] + product[1, ..., :width])


def twist(factor, real, imag):
    return (factor[0] * real - factor[1] * imag, factor[0] * imag + factor[1] * real)


def to_bf16(pair):
    return tuple(part.astype(jnp.bfloat16) for part in pair)


def to_f32(pair):
    return tuple(part.astype(jnp.float32) for part in pair)


def body(rhs_field, panel_inverse, coupling):
    planes = lax.axis_size("plane")
    layers = lax.axis_size("layer")
    place = lax.axis_index("layer")
    plane = lax.axis_index("plane")
    pairs = layers // 2

    block = rhs_field[0]
    parts, loads, ys, chunk = block.shape
    block = block.reshape(parts, loads, planes, ys // planes, chunk)
    block = jnp.moveaxis(block, 2, 0)
    block = lax.all_to_all(block, "plane", split_axis=0, concat_axis=0, tiled=True)
    lines = jnp.moveaxis(block, 0, 3).reshape(parts, loads, ys // planes, planes * chunk)

    inverse = panel_inverse[0]
    factors = coupling[0][..., None]
    width = inverse.shape[0]
    down = [(2 * j + 1, 2 * j) for j in range(pairs)]
    back = [(2 * j, 2 * j + 1) for j in range(pairs)]

    rows = width // planes
    piece = lax.dynamic_slice_in_dim(inverse, plane * rows, rows, 0)
    piece = lax.ppermute(piece, "layer", down)
    inverse_next = lax.all_gather(piece, "plane", axis=0, tiled=True)
    lines_next = lax.ppermute(lines, "layer", down)
    factors_next = lax.ppermute(factors, "layer", down)

    def mix(source, factor, carried):
        twisted = twist(factor, *to_f32(carried))
        return to_bf16((source[0] + twisted[0], source[1] + twisted[1]))

    def pair_forward(incoming):
        first = complex_product(*mix(lines, factors, (incoming[0], incoming[1])), inverse)
        second = complex_product(*mix(lines_next, factors_next, to_bf16(first)), inverse_next)
        return first, second

    zero = jnp.zeros(lines.shape[1:], jnp.float32)
    outgoing = jnp.zeros(lines.shape, jnp.bfloat16)
    store_a, store_b = (zero, zero), (zero, zero)
    for section in range(pairs):
        if section > 0:
            incoming = lax.ppermute(outgoing, "layer", [(2 * section - 2, 2 * section)])
        else:
            incoming = outgoing

        def active(incoming, store_a, store_b, outgoing):
            first, second = pair_forward(incoming)
            return first, second, jnp.stack(to_bf16(second))

        def idle(incoming, store_a, store_b, outgoing):
            return store_a, store_b, outgoing

        store_a, store_b, outgoing = lax.cond(
            place == 2 * section, active, idle, incoming, store_a, store_b, outgoing)

    def pair_backward(sweep_b):
        carried = to_bf16(twist(factors_next, *sweep_b))
        product = complex_product(*carried, inverse)
        sweep_a = (store_a[0] + product[0], store_a[1] + product[1])
        return sweep_a, jnp.stack(to_bf16(twist(factors, *sweep_a)))

    result_a, result_b = (zero, zero), (zero, zero)
    for section in range(pairs):
        lead = layers - 2 - 2 * section
        if section > 0:
            incoming = lax.ppermute(outgoing, "layer", [(lead + 2, lead)])
        else:
            incoming = outgoing

        def active(incoming, result_a, result_b, outgoing, first=(section == 0)):
            if first:
                sweep_b = store_b
            else:
                product = complex_product(incoming[0], incoming[1], inverse_next)
                sweep_b = (store_b[0] + product[0], store_b[1] + product[1])
            sweep_a, outgoing = pair_backward(sweep_b)
            return sweep_a, sweep_b, outgoing

        def idle(incoming, result_a, result_b, outgoing):
            return result_a, result_b, outgoing

        result_a, result_b, outgoing = lax.cond(
            place == lead, active, idle, incoming, result_a, result_b, outgoing)

    returned = lax.ppermute(jnp.stack(result_b), "layer", back)
    result = jnp.where(place % 2 == 0, jnp.stack(result_a), returned)

    result = result.reshape(parts, loads, ys // planes, planes, chunk)
    result = jnp.moveaxis(result, 3, 0)
    result = lax.all_to_all(result, "plane", split_axis=0, concat_axis=0, tiled=True)
    result = jnp.moveaxis(result, 0, 2).reshape(parts, loads, ys, chunk)
    return result[None]


def solution(mesh):
    in_specs = (
        P("layer", None, None, None, "plane"),
        P("layer", None, None),
        P("layer", None, None, "plane"),
    )
    out_specs = P("layer", None, None, None, "plane")
    return jax.shard_map(body, mesh=mesh, in_specs=in_specs, out_specs=out_specs, check_vma=False)
```

time: 514 us -> 508 us (0.988)
  local copies, waits for them, and re-layouts: 26.1 us -> 6.38 us
  waiting for transfers between devices: 399 us -> 418 us
    ppermute x1, waiting for transfers between devices: 369 us -> 388 us  [body(): returned = lax.ppermute(jnp.stack(result_b), 'layer', back)]
    unnamed x5 -> x2, local copies, waits for them, and re-layouts: 15.4 us -> 0.86 us
where the time goes in v3:
time: 508 us; the launch traced here: 499 us
  waiting for transfers between devices  418 us (82%)
  starting transfers between devices  31.1 us (6%)
  blocking collectives  22.6 us (4%)
  between operations  14.7 us (3%)
  local copies, waits for them, and re-layouts  6.38 us (1%)
    ppermute x1, waiting for transfers between devices, body(): returned = lax.ppermute(jnp.stack(result_b), 'layer', back)  388 us
    all_gather x1, waiting for transfers between devices, body(): inverse_next = lax.all_gather(piece, 'plane', axis=0, tiled=True)  17.4 us
    all_to_all x1, blocking collectives, body(): lax.all_to_all(block, 'plane', split_axis=0, concat_axis=0, tiled=True)  12.4 us
    all_to_all x1, blocking collectives, body(): lax.all_to_all(result, 'plane', split_axis=0, concat_axis=0, tiled=True)  10.2 us
  transfers between devices with their start and end apart: 35, of which 4 were waited for; matrix products, arithmetic and copies ran while one was open for 0% of the time, Pallas kernels for 0%

profile of v3, /device:TPU:8, one launch (start us, length us, event | category | flops | bytes accessed | tf_op | source)
XLA Modules:
  0.0 499.2 jit_solution(17778963696012328530)
XLA Ops:
  6.5 1.1 dynamic-slice_bitcast_fusion
  7.6 4.1 collective-permute-start.2
  11.7 8.6 %collective-permute-done.2 = bf16[128,2048]{1,0:T(8,128)(2,1)S(1)} collective-permute-done((bf16[128,2048]{1,0:T(8,128)(2,1)S(1)}, bf16[128,2048]{1,0:T(8,128)(2,1)S(1)}, u32[]{:S(2)}, u32[]{:S(2)}) %collective-permute-start.2) | collective-permute-done | bytes 524320 | tf_op jit(solution)/shard_map/ppermute | solution.py:51
  20.4 0.9 copy-done.31
  21.2 1.0 copy.130
  22.2 12.4 %all_to_all.10 = f32[8,2,4,8,128]{4,3,2,1,0:T(8,128)S(1)} all-to-all(f32[8,2,4,8,128]{4,3,2,1,0:T(8,128)S(1)} %copy.130), channel_id=1, replica_groups=mesh['layer'=32,'plane'=8] {'plane'}, dimensions={0} | all-to-all | bytes 524288 | tf_op jit(solution)/shard_map/all_to_all | solution.py:40
  34.6 4.4 collective-permute-start
  39.0 1.3 collective-permute-start.1
  40.3 3.9 collective-permute-done.1
  44.3 17.4 %all-gather.2.cloned.1.call-done = bf16[1024,2048]{1,0:T(8,128)(2,1)} async-done(((bf16[128,2048]{1,0:T(8,128)(2,1)}), bf16[1024,2048]{1,0:T(8,128)(2,1)}) %all-gather.2.cloned.1.call-update) | async-done | bytes 4194320 | tf_op jit(solution)/shard_map/all_gather | solution.py:52
  61.8 0.7 collective-permute-start.3
  62.5 0.7 collective-permute-start.4
  63.2 0.7 collective-permute-start.5
  63.9 0.7 collective-permute-start.6
  64.6 0.7 collective-permute-start.7
  65.3 0.7 collective-permute-start.8
  67.2 0.7 collective-permute-start.10
  67.9 0.7 collective-permute-start.11
  70.0 0.7 collective-permute-start.14
  72.1 3.4 conditional.46
  75.5 0.7 collective-permute-start.17
  76.2 2.7 conditional.48
  76.9 0.7 broadcast.144.clone.1
  79.6 0.7 collective-permute-start.19
  84.7 0.7 collective-permute-start.26
  85.4 0.7 collective-permute-start.27
  89.9 1.0 pad_maximum_fusion.31
  90.9 1.3 collective-permute-start.33
  92.2 387.7 %collective-permute-done.33 = f32[2,4,8,1024]{3,2,1,0:T(8,128)S(1)} collective-permute-done((f32[2,4,8,1024]{3,2,1,0:T(8,128)S(1)}, f32[2,4,8,1024]{3,2,1,0:T(8,128)S(1)}, u32[]{:S(2)}, u32[]{:S(2)}) %collective-permute-start.33) | collective-permute-done | bytes 262176 | tf_op jit(solution)/shard_map/ppermute | solution.py:113
  479.9 1.0 fusion.912
  480.9 10.2 %all_to_all.11 = f32[8,2,4,8,128]{4,3,2,1,0:T(8,128)S(1)} all-to-all(f32[8,2,4,8,128]{4,3,2,1,0:T(8,128)S(1)} %copy.195), channel_id=1, replica_groups=mesh['layer'=32,'plane'=8] {'plane'}, dimensions={0} | all-to-all | bytes 524288 | tf_op jit(solution)/shard_map/all_to_all | solution.py:118
  491.2 0.7 copy.265
  (91 shorter events, 14.8 us)
Async XLA Ops:
  6.5 55.1 %all-gather.2.cloned.1.call-start = ((), (), s32[]{:S(2)}) async-start(), calls=%async_computation.2 | async-start | bytes 4718592 | tf_op jit(solution)/shard_map/all_gather | solution.py:52
  7.6 12.7 %collective-permute-start.2 = (bf16[128,2048]{1,0:T(8,128)(2,1)S(1)}, bf16[128,2048]{1,0:T(8,128)(2,1)S(1)}, u32[]{:S(2)}, u32[]{:S(2)}) collective-permute-start(bf16[128,2048]{1,0:T(8,128)(2,1)S(1)} %dynamic-slice_bitcast_fusion), channel_id=1, source_target_pairs={{8,0},{24,16},{40,32},{56,48},{72,64},{88,80},{104,96},{120,112},{... | collective-permute-start | bytes 1572872 | tf_op jit(solution)/shard_map/ppermute | solution.py:51
  34.6 9.7 %collective-permute-start = (f32[2,4,8,1024]{3,2,1,0:T(8,128)S(1)}, f32[2,4,8,1024]{3,2,1,0:T(8,128)S(1)}, u32[]{:S(2)}, u32[]{:S(2)}) collective-permute-start(f32[2,4,8,1024]{3,2,1,0:T(8,128)S(1)} %copy_bitcast_fusion), channel_id=1, source_target_pairs={{8,0},{24,16},{40,32},{56,48},{72,64},{88,80},{104,96},{120,112},{... | collective-permute-start | bytes 786440 | tf_op jit(solution)/shard_map/ppermute | solution.py:53
  39.0 5.3 %collective-permute-start.1 = (f32[2,4,8,1]{2,1,0,3:T(4,128)}, f32[2,4,8,1]{2,1,0,3:T(4,128)S(1)}, u32[]{:S(2)}, u32[]{:S(2)}) collective-permute-start(f32[2,4,8,1]{2,1,0,3:T(4,128)} %bitcast.1311), channel_id=1, source_target_pairs={{8,0},{24,16},{40,32},{56,48},{72,64},{88,80},{104,96},{120,112},{... | collective-permute-start | bytes 776 | tf_op jit(solution)/shard_map/ppermute | solution.py:54
  61.8 0.7 collective-permute-start.3
  62.5 0.7 collective-permute-start.4
  63.2 0.7 collective-permute-start.5
  63.9 0.7 collective-permute-start.6
  64.6 0.7 collective-permute-start.7
  65.3 0.7 collective-permute-start.8
  66.0 0.7 collective-permute-start.9
  67.2 0.7 collective-permute-start.10
  67.9 0.7 collective-permute-start.11
  68.6 0.7 collective-permute-start.12
  69.3 0.7 collective-permute-start.13
  70.0 0.7 collective-permute-start.14
  70.7 0.7 collective-permute-start.15
  71.4 0.7 collective-permute-start.16
  75.5 0.7 collective-permute-start.17
  79.6 0.7 collective-permute-start.19
  80.3 0.7 collective-permute-start.20
  81.0 0.7 collective-permute-start.21
  81.7 0.7 collective-permute-start.22
  82.4 0.7 collective-permute-start.23
  83.3 0.7 collective-permute-start.24
  84.0 0.7 collective-permute-start.25
  84.7 0.7 collective-permute-start.26
  85.4 0.7 collective-permute-start.27
  86.1 0.7 collective-permute-start.28
  86.8 0.7 collective-permute-start.29
  88.5 0.7 collective-permute-start.31
  90.9 389.0 %collective-permute-start.33 = (f32[2,4,8,1024]{3,2,1,0:T(8,128)S(1)}, f32[2,4,8,1024]{3,2,1,0:T(8,128)S(1)}, u32[]{:S(2)}, u32[]{:S(2)}) collective-permute-start(f32[2,4,8,1024]{3,2,1,0:T(8,128)S(1)} %pad_maximum_fusion.31), channel_id=1, source_target_pairs={{0,8},{16,24},{32,40},{48,56},{64,72},{80,88},{96,104},{112,120},{... | collective-permute-start | bytes 786440 | tf_op jit(solution)/shard_map/ppermute | solution.py:113
  (4 other events, 2.9 us)
Sparse Core Ops, SparseCore 0:
  21.4 40.2 all-gather.1
